TPU v7x, 512 devices: a whole 4x4x16 slice. The times are simulated.
512 devices in a mesh: tile: 64 (over z, x_hi, core), chan: 8 (over x_lo, y).
Axes of the slice: x: 4 (x_hi: 2, x_lo: 2; x = x_hi * 2 + x_lo), y: 4, z: 16, core: 2. Of those that a mesh axis runs over, the one named last changes fastest.
Arguments:
- analysis: bfloat16 [64, 524288], P('chan', 'tile'), may hold values from -6 to 6
- send_rows: int32 [64, 5, 128], P('tile'), may hold values from 0 to 8191
- send_count: int32 [64, 5], P('tile'), may hold values from 64 to 128, as said below
- corner_slot: int32 [4, 2048, 256], P(None, 'tile'), may hold values from 0 to 639, as said below
- corner_weight: float32 [4, 2048, 256], P(None, 'tile'), may hold values from 0.1 to 0.6
- beside: int32 [2048, 8], P('tile'), may hold values from 0 to 2047, as said below
- quarter_turns: int32 [2048, 8], P('tile'), may hold values from 0 to 3
- kernel_one: bfloat16 [9, 128, 64], P(None, 'chan'), may hold values from -0.375 to 0.375
- kernel_two: bfloat16 [9, 128, 128], P(None, 'chan'), may hold values from -0.25 to 0.25
- kernel_three: bfloat16 [9, 128, 128], P(None, 'chan'), may hold values from -0.25 to 0.25
Outputs:
- forecast: bfloat16 [128, 2048, 256], P('chan', 'tile')
Inputs may be any that keep to these rules, and one draw needn't show every extreme that they name: send_count[s, d] is at least 64; every shard sends 128 to itself (d = 2), and some receiver gets 128 from each of its 5 senders. corner_slot[j, t, i] = d * 128 + k names a live slot, k < send_count[s, d], of the block that shard s = (e - d + 2) mod the shard count sends to the shard e holding tile t; the four corners of a pixel are slots k, k + 1, k + 2, k + 3 of one block. beside[t, k] = (t + d) mod 2048 with 1 <= |d| <= 2.
All inputs are finite; a program needn't handle non-finite values.
Results may differ from a plain program's by a relative error of at most 0.007.
Values may be sent and summed in bfloat16 or wider, within the bound.
No kernel may reach another device: no remote copies, remote signals or barrier semaphores. Data moves between devices by JAX's collectives and lax.ppermute only.
A program may use at most 64 MiB of HBM per device.

v0:
```python
import jax
import jax.numpy as jnp
import numpy as np
from jax import lax
from jax.sharding import PartitionSpec as P

P_SIZE = 16
REACH = 2


def from_behind(value, axis, steps):
    count = lax.axis_size(axis)
    pairs = [(source, (source + steps) % count) for source in range(count)]
    return lax.ppermute(value, axis, pairs)


def extended_2(x, sides, width):
    for axis, dim in sides:
        size, length = (lax.axis_size(axis), x.shape[dim])
        up = [(i, (i + 1) % size) for i in range(size)]
        down = [(j, i) for i, j in up]
        last = lax.slice_in_dim(x, length - width, length, axis=dim)
        initial = lax.slice_in_dim(x, 0, width, axis=dim)
        before = lax.ppermute(last, axis, up)
        after = lax.ppermute(initial, axis, down)
        x = jnp.concatenate([before, x, after], axis=dim)
    return x


def cycle_table(extent):
    length = 4 * extent - 4
    entries = []
    for cycle_pos in range(length):
        if cycle_pos < extent:
            row_at, col_at = (cycle_pos, 0)
        elif cycle_pos < 2 * extent - 1:
            row_at, col_at = (extent - 1, cycle_pos - extent + 1)
        elif cycle_pos < 3 * extent - 2:
            row_at, col_at = (3 * extent - 3 - cycle_pos, extent - 1)
        else:
            row_at, col_at = (0, 4 * extent - 4 - cycle_pos)
        entries.append(row_at * extent + col_at)
    return np.array(entries, np.int32)


def border_tables(extent):
    length = 4 * extent - 4
    heading = []
    anchor = []
    for col_at in range(extent):
        heading.append(0)
        anchor.append(extent - 1 + col_at)
    for col_at in range(extent):
        heading.append(1)
        anchor.append((length - col_at) % length)
    for row_at in range(extent):
        heading.append(2)
        anchor.append(3 * extent - 3 - row_at)
    for row_at in range(extent):
        heading.append(3)
        anchor.append(row_at)
    heading += [4, 5, 6, 7]
    anchor += [2 * extent - 2, extent - 1, 3 * extent - 3, 0]
    return (np.array(heading, np.int32), np.array(anchor, np.int32))


def layout_table(extent):
    padded_side = extent + 2
    interior = extent * extent
    entries = []
    for row_at in range(padded_side):
        for col_at in range(padded_side):
            if 1 <= row_at <= extent and 1 <= col_at <= extent:
                entries.append((row_at - 1) * extent + col_at - 1)
            elif row_at == 0 and 1 <= col_at <= extent:
                entries.append(interior + col_at - 1)
            elif row_at == padded_side - 1 and 1 <= col_at <= extent:
                entries.append(interior + extent + col_at - 1)
            elif col_at == 0 and 1 <= row_at <= extent:
                entries.append(interior + 2 * extent + row_at - 1)
            elif col_at == padded_side - 1 and 1 <= row_at <= extent:
                entries.append(interior + 3 * extent + row_at - 1)
            else:
                corner = (0 if row_at == 0 else 2) + (0 if col_at == 0 else 1)
                entries.append(interior + 4 * extent + corner)
    return np.array(entries, np.int32)


def conv_layer(activity, kernel, local_beside, local_turns, gather_rims):
    length = 4 * P_SIZE - 4
    cycle_vals = jnp.take(activity, cycle_table(P_SIZE), axis=2)
    extended = gather_rims(cycle_vals)
    heading, anchor = border_tables(P_SIZE)
    near_tile = jnp.take(local_beside, heading, axis=1)
    near_turn = jnp.take(local_turns, heading, axis=1)
    source = near_tile * length + jnp.remainder(anchor[None, :] - near_turn * (P_SIZE - 1), length)
    flat_cycles = extended.reshape(extended.shape[0], -1)
    border = jnp.take(flat_cycles, source.reshape(-1), axis=1)
    border = border.reshape(activity.shape[0], activity.shape[1], 4 * P_SIZE + 4)
    joined = jnp.concatenate([activity, border], axis=2)
    padded = jnp.take(joined, layout_table(P_SIZE), axis=2)
    padded_side = P_SIZE + 2
    stretch = P_SIZE * padded_side - 2
    summed = None
    for tap_index in range(9):
        offset = padded_side + 1 + (tap_index // 3 - 1) * padded_side + (tap_index % 3 - 1)
        window = padded[:, :, offset : offset + stretch]
        partial_sum = jnp.einsum(
            "oc,ctq->otq", kernel[tap_index], window, preferred_element_type=jnp.float32
        )
        summed = partial_sum if summed is None else summed + partial_sum
    summed = jnp.pad(summed, ((0, 0), (0, 0), (0, 2)))
    summed = summed.reshape(summed.shape[0], summed.shape[1], P_SIZE, padded_side)[:, :, :, :P_SIZE]
    summed = summed.reshape(summed.shape[0], summed.shape[1], P_SIZE * P_SIZE)
    return jax.nn.gelu(summed, approximate=False).astype(jnp.bfloat16)


def on_device(
    analysis,
    send_rows,
    send_count,
    corner_slot,
    corner_weight,
    beside,
    quarter_turns,
    kernel_one,
    kernel_two,
    kernel_three,
):
    shards = lax.axis_size("tile")
    groups = lax.axis_size("chan")
    tiles_here = corner_slot.shape[1]
    near_count = send_rows.shape[1]
    capacity = send_rows.shape[2]
    channels_here = analysis.shape[0]
    pixels = corner_slot.shape[2]
    total_tiles = tiles_here * shards
    per_group = tiles_here // groups
    widths = [kernel_one.shape[2], kernel_two.shape[2], kernel_three.shape[2]]
    joined_kernels = jnp.concatenate([kernel_one, kernel_two, kernel_three], axis=2)
    joined_kernels = lax.all_gather(joined_kernels, "chan", axis=1, tiled=True)
    kernels = []
    low = 0
    for width in widths:
        kernels.append(joined_kernels[:, :, low : low + width])
        low += width
    slot_order = jnp.arange(capacity)
    rows_list = send_rows[0].reshape(-1)
    piece = jnp.take(analysis, rows_list, axis=1).reshape(channels_here, near_count, capacity)
    is_live = slot_order[None, :] < send_count[0][:, None]
    piece = jnp.where(is_live[None], piece, jnp.zeros((), piece.dtype))
    blocks = []
    for offset_index in range(near_count):
        block = piece[:, offset_index]
        if offset_index != REACH:
            block = from_behind(block, "tile", offset_index - REACH)
        blocks.append(block)
    arrived = jnp.stack(blocks, axis=1).reshape(channels_here, near_count * capacity)
    arrived = lax.all_gather(arrived, "chan", axis=0, tiled=True)
    group_index = lax.axis_index("chan")
    my_slots = lax.dynamic_slice_in_dim(corner_slot, group_index * per_group, per_group, 1)
    my_weights = lax.dynamic_slice_in_dim(corner_weight, group_index * per_group, per_group, 1)
    my_slots = my_slots.reshape(my_slots.shape[0], per_group * pixels)
    my_weights = my_weights.reshape(my_weights.shape[0], per_group * pixels)
    slot_ids = jnp.arange(near_count * capacity)
    summed = None
    for corner in range(my_slots.shape[0]):
        one_hot = (slot_ids[:, None] == my_slots[corner][None, :]).astype(arrived.dtype)
        picked = jnp.dot(arrived, one_hot, preferred_element_type=jnp.float32)
        term = picked * my_weights[corner][None, :]
        summed = term if summed is None else summed + term
    activity = summed.astype(jnp.bfloat16).reshape(arrived.shape[0], per_group, pixels)
    first_tile = lax.axis_index(("tile", "chan")) * per_group
    near_beside = lax.dynamic_slice_in_dim(beside, group_index * per_group, per_group, 0)
    near_turns = lax.dynamic_slice_in_dim(quarter_turns, group_index * per_group, per_group, 0)
    local_beside = jnp.remainder(near_beside - first_tile + REACH, total_tiles)

    def joined_rims(cycle_vals):
        return extended_2(cycle_vals, ((("tile", "chan"), 1),), REACH)

    for kernel in kernels:
        activity = conv_layer(activity, kernel, local_beside, near_turns, joined_rims)
    result = lax.all_to_all(activity, "chan", split_axis=0, concat_axis=1, tiled=True)
    return result


def solution(mesh):
    return jax.shard_map(
        on_device,
        mesh=mesh,
        in_specs=(
            P("chan", "tile"),
            P("tile", None, None),
            P("tile", None),
            P(None, "tile", None),
            P(None, "tile", None),
            P("tile", None),
            P("tile", None),
            P(None, "chan", None),
            P(None, "chan", None),
            P(None, "chan", None),
        ),
        out_specs=P("chan", "tile", None),
        check_vma=False,
    )
```

profile of v0, /device:TPU:2, one launch (start us, length us, event | category | flops | bytes accessed | tf_op | source)
XLA Modules:
  0.0 177.2 jit_solution(4643471819461875339)
XLA Ops:
  0.1 0.8 fusion.74
  0.8 0.8 iota_compare_fusion.24
  1.6 1.9 %copy.243 = bf16[8,8192]{0,1:T(8,128)(2,1)S(1)} copy(bf16[8,8192]{1,0:T(8,128)(2,1)} %param.30) | data formatting | bytes 262144 | tf_op args[0]
  3.5 2.0 %gather_fusion = bf16[640,8]{1,0:T(8,128)(2,1)S(1)} fusion(bf16[8,8192]{0,1:T(8,128)(2,1)S(1)} %copy.243, s32[1024]{0:T(1024)S(1)} %pad_clamp_fusion.5), kind=kCustom, calls=%fused_computation.8 | custom fusion | bytes 23040 | tf_op jit(solution)/shard_map/jit(_take)/gather | solution.py:149
  5.6 13.0 %collective-permute-start = (bf16[8,128]{1,0:T(8,128)(2,1)S(1)}, bf16[8,128]{1,0:T(8,128)(2,1)S(1)}, u32[]{:S(2)}, u32[]{:S(2)}) collective-permute-start(bf16[8,128]{1,0:T(8,128)(2,1)S(1)} %get-tuple-element.35), channel_id=1, source_target_pairs={{0,496},{8,504},{16,0},{24,8},{32,16},{40,24},{48,32},{56,40},{64,... | collective-permute-start | bytes 6152 | tf_op jit(solution)/shard_map/ppermute | solution.py:14
  18.6 2.5 %collective-permute-start.1 = (bf16[8,128]{1,0:T(8,128)(2,1)S(1)}, bf16[8,128]{1,0:T(8,128)(2,1)S(1)}, u32[]{:S(2)}, u32[]{:S(2)}) collective-permute-start(bf16[8,128]{1,0:T(8,128)(2,1)S(1)} %get-tuple-element.34), channel_id=1, source_target_pairs={{0,504},{8,0},{16,8},{24,16},{32,24},{40,32},{48,40},{56,48},{64,5... | collective-permute-start | bytes 6152 | tf_op jit(solution)/shard_map/ppermute | solution.py:14
  24.5 29.9 %all_gather.6 = bf16[9,128,320]{2,1,0:T(8,128)(2,1)S(1)} all-gather(bf16[9,16,320]{2,1,0:T(8,128)(2,1)S(1)} %pad_maximum_fusion.6), channel_id=1, replica_groups=mesh['tile'=64,'chan'=8] {'chan'}, dimensions={1}, use_global_device_ids=true | all-gather | bytes 829440 | tf_op jit(solution)/shard_map/all_gather | solution.py:141
  54.5 1.9 %collective-permute-start.2 = (bf16[8,128]{1,0:T(8,128)(2,1)S(1)}, bf16[8,128]{1,0:T(8,128)(2,1)S(1)}, u32[]{:S(2)}, u32[]{:S(2)}) collective-permute-start(bf16[8,128]{1,0:T(8,128)(2,1)S(1)} %get-tuple-element.32), channel_id=1, source_target_pairs={{0,8},{8,16},{16,24},{24,32},{32,40},{40,48},{48,56},{56,64},{64,7... | collective-permute-start | bytes 6152 | tf_op jit(solution)/shard_map/ppermute | solution.py:14
  56.6 3.5 %collective-permute-start.3 = (bf16[8,128]{1,0:T(8,128)(2,1)S(1)}, bf16[8,128]{1,0:T(8,128)(2,1)S(1)}, u32[]{:S(2)}, u32[]{:S(2)}) collective-permute-start(bf16[8,128]{1,0:T(8,128)(2,1)S(1)} %get-tuple-element.31), channel_id=1, source_target_pairs={{0,16},{8,24},{16,32},{24,40},{32,48},{40,56},{48,64},{56,72},{64,... | collective-permute-start | bytes 6152 | tf_op jit(solution)/shard_map/ppermute | solution.py:14
  60.1 2.9 %collective-permute-done.2 = bf16[8,128]{1,0:T(8,128)(2,1)S(1)} collective-permute-done((bf16[8,128]{1,0:T(8,128)(2,1)S(1)}, bf16[8,128]{1,0:T(8,128)(2,1)S(1)}, u32[]{:S(2)}, u32[]{:S(2)}) %collective-permute-start.2) | collective-permute-done | bytes 2080 | tf_op jit(solution)/shard_map/ppermute | solution.py:14
  63.1 2.6 %collective-permute-done.3 = bf16[8,128]{1,0:T(8,128)(2,1)S(1)} collective-permute-done((bf16[8,128]{1,0:T(8,128)(2,1)S(1)}, bf16[8,128]{1,0:T(8,128)(2,1)S(1)}, u32[]{:S(2)}, u32[]{:S(2)}) %collective-permute-start.3) | collective-permute-done | bytes 2080 | tf_op jit(solution)/shard_map/ppermute | solution.py:14
  65.7 28.2 %all_gather.7 = bf16[64,640]{1,0:T(8,128)(2,1)S(1)} all-gather(bf16[8,640]{1,0:T(8,128)(2,1)S(1)} %bitcast.272), channel_id=1, replica_groups=mesh['tile'=64,'chan'=8] {'chan'}, dimensions={0}, use_global_device_ids=true | all-gather | bytes 92160 | tf_op jit(solution)/shard_map/all_gather | solution.py:159
  97.3 3.2 %collective-permute-start.4 = (bf16[64,2,60]{0,1,2:T(2,128)(2,1)S(1)}, bf16[64,2,60]{0,1,2:T(2,128)(2,1)S(1)}, u32[]{:S(2)}, u32[]{:S(2)}) collective-permute-start(bf16[64,2,60]{0,1,2:T(2,128)(2,1)S(1)} %get-tuple-element.29), channel_id=1, source_target_pairs={{0,1},{1,2},{2,3},{3,4},{4,5},{5,6},{6,7},{7,8},{8,9},{9,10},{10,1... | collective-permute-start | bytes 46088 | tf_op jit(solution)/shard_map/ppermute | solution.py:24
  100.6 4.9 %collective-permute-start.5 = (bf16[64,2,60]{0,1,2:T(2,128)(2,1)S(1)}, bf16[64,2,60]{0,1,2:T(2,128)(2,1)S(1)}, u32[]{:S(2)}, u32[]{:S(2)}) collective-permute-start(bf16[64,2,60]{0,1,2:T(2,128)(2,1)S(1)} %get-tuple-element.30), channel_id=1, source_target_pairs={{1,0},{2,1},{3,2},{4,3},{5,4},{6,5},{7,6},{8,7},{9,8},{10,9},{11,1... | collective-permute-start | bytes 46088 | tf_op jit(solution)/shard_map/ppermute | solution.py:25
  105.7 1.2 collective-permute-done.5
  107.1 1.4 gather_fusion.2
  108.9 2.0 %gather_fusion.3 = bf16[324,64,4]{1,2,0:T(4,128)(2,1)S(1)} fusion(bf16[64,4,324]{0,1,2:T(4,128)(2,1)S(1)} %pad_maximum_fusion.2, s32[1024]{0:T(1024)S(1)} %get-tuple-element.37), kind=kCustom, calls=%fused_computation.11 | custom fusion | bytes 333072 | tf_op jit(solution)/shard_map/jit(_take)/gather | solution.py:101
  116.9 1.1 fusion.18
  118.9 2.6 %collective-permute-start.6 = (bf16[128,2,60]{0,1,2:T(2,128)(2,1)S(1)}, bf16[128,2,60]{0,1,2:T(2,128)(2,1)S(1)}, u32[]{:S(2)}, u32[]{:S(2)}) collective-permute-start(bf16[128,2,60]{0,1,2:T(2,128)(2,1)S(1)} %get-tuple-element.27), channel_id=1, source_target_pairs={{0,1},{1,2},{2,3},{3,4},{4,5},{5,6},{6,7},{7,8},{8,9},{9,10},{10,1... | collective-permute-start | bytes 92168 | tf_op jit(solution)/shard_map/ppermute | solution.py:24
  121.5 5.9 %collective-permute-start.7 = (bf16[128,2,60]{0,1,2:T(2,128)(2,1)S(1)}, bf16[128,2,60]{0,1,2:T(2,128)(2,1)S(1)}, u32[]{:S(2)}, u32[]{:S(2)}) collective-permute-start(bf16[128,2,60]{0,1,2:T(2,128)(2,1)S(1)} %get-tuple-element.28), channel_id=1, source_target_pairs={{1,0},{2,1},{3,2},{4,3},{5,4},{6,5},{7,6},{8,7},{9,8},{10,9},{11,1... | collective-permute-start | bytes 92168 | tf_op jit(solution)/shard_map/ppermute | solution.py:25
  127.4 1.3 collective-permute-done.7
  128.9 1.4 gather_fusion.7
  130.9 2.0 %gather_fusion.8 = bf16[324,128,4]{1,2,0:T(4,128)(2,1)S(1)} fusion(bf16[128,4,324]{0,1,2:T(4,128)(2,1)S(1)} %copy.275, s32[1024]{0:T(1024)S(1)} %get-tuple-element.37), kind=kCustom, calls=%fused_computation.3.clone | custom fusion | bytes 664848 | tf_op jit(solution)/shard_map/jit(_take)/gather | solution.py:101
  137.0 1.1 fusion.21
  139.0 2.5 %collective-permute-start.8 = (bf16[128,2,60]{0,1,2:T(2,128)(2,1)S(1)}, bf16[128,2,60]{0,1,2:T(2,128)(2,1)S(1)}, u32[]{:S(2)}, u32[]{:S(2)}) collective-permute-start(bf16[128,2,60]{0,1,2:T(2,128)(2,1)S(1)} %get-tuple-element.25), channel_id=1, source_target_pairs={{0,1},{1,2},{2,3},{3,4},{4,5},{5,6},{6,7},{7,8},{8,9},{9,10},{10,1... | collective-permute-start | bytes 92168 | tf_op jit(solution)/shard_map/ppermute | solution.py:24
  141.5 5.8 %collective-permute-start.9 = (bf16[128,2,60]{0,1,2:T(2,128)(2,1)S(1)}, bf16[128,2,60]{0,1,2:T(2,128)(2,1)S(1)}, u32[]{:S(2)}, u32[]{:S(2)}) collective-permute-start(bf16[128,2,60]{0,1,2:T(2,128)(2,1)S(1)} %get-tuple-element.26), channel_id=1, source_target_pairs={{1,0},{2,1},{3,2},{4,3},{5,4},{6,5},{7,6},{8,7},{9,8},{10,9},{11,1... | collective-permute-start | bytes 92168 | tf_op jit(solution)/shard_map/ppermute | solution.py:25
  147.3 1.5 collective-permute-done.9
  149.0 1.4 gather_fusion.10
  151.0 2.0 %gather_fusion.11 = bf16[324,128,4]{1,2,0:T(4,128)(2,1)S(1)} fusion(bf16[128,4,324]{0,1,2:T(4,128)(2,1)S(1)} %copy.289, s32[1024]{0:T(1024)S(1)} %get-tuple-element.37), kind=kCustom, calls=%fused_computation.7.clone | custom fusion | bytes 664848 | tf_op jit(solution)/shard_map/jit(_take)/gather | solution.py:101
  157.2 1.1 fusion.24
  158.5 17.9 %all_to_all.18 = bf16[128,4,256]{2,1,0:T(4,128)(2,1)S(1)} all-to-all(bf16[128,4,256]{2,1,0:T(4,128)(2,1)S(1)} %copy.300), channel_id=1, replica_groups=mesh['tile'=64,'chan'=8] {'chan'}, dimensions={0} | all-to-all | bytes 524288 | tf_op jit(solution)/shard_map/all_to_all | solution.py:183
  176.4 0.8 copy.303
  (146 shorter events, 25.2 us)
Async XLA Ops:
  0.0 21.9 %copy-start = (s32[32,8]{0,1:T(8,128)S(1)}, s32[32,8]{0,1:T(8,128)}, u32[]{:S(2)}) copy-start(s32[32,8]{0,1:T(8,128)} %param.36) | copy-start | bytes 3076
  0.0 21.1 %copy-start.7 = (s32[68]{0:T(128)S(1)}, s32[68]{0:T(128)}, u32[]{:S(2)}) copy-start(s32[68]{0:T(128)} %constant.310) | copy-start | bytes 820
  0.0 22.7 %copy-start.6 = (s32[68]{0:T(128)S(1)}, s32[68]{0:T(128)}, u32[]{:S(2)}) copy-start(s32[68]{0:T(128)} %constant.243) | copy-start | bytes 820
  0.0 56.5 %copy-start.8 = (s32[60]{0:T(128)S(1)}, s32[60]{0:T(128)}, u32[]{:S(2)}) copy-start(s32[60]{0:T(128)} %constant.221.clone) | copy-start | bytes 724
  0.0 21.1 %copy-start.4 = (s32[32,8]{0,1:T(8,128)S(1)}, s32[32,8]{0,1:T(8,128)}, u32[]{:S(2)}) copy-start(s32[32,8]{0,1:T(8,128)} %param.35) | copy-start | bytes 3076
  0.0 24.3 %copy-start.3 = (bf16[9,16,64]{2,1,0:T(8,128)(2,1)S(1)}, bf16[9,16,64]{2,1,0:T(8,128)(2,1)}, u32[]{:S(2)}) copy-start(bf16[9,16,64]{2,1,0:T(8,128)(2,1)} %param.37) | copy-start | bytes 55300
  0.0 24.3 %copy-start.2 = (bf16[9,16,128]{2,1,0:T(8,128)(2,1)S(1)}, bf16[9,16,128]{2,1,0:T(8,128)(2,1)}, u32[]{:S(2)}) copy-start(bf16[9,16,128]{2,1,0:T(8,128)(2,1)} %param.38) | copy-start | bytes 110596
  0.1 24.3 %copy-start.1 = (bf16[9,16,128]{2,1,0:T(8,128)(2,1)S(1)}, bf16[9,16,128]{2,1,0:T(8,128)(2,1)}, u32[]{:S(2)}) copy-start(bf16[9,16,128]{2,1,0:T(8,128)(2,1)} %param.39) | copy-start | bytes 110596
  5.6 48.8 %collective-permute-start = (bf16[8,128]{1,0:T(8,128)(2,1)S(1)}, bf16[8,128]{1,0:T(8,128)(2,1)S(1)}, u32[]{:S(2)}, u32[]{:S(2)}) collective-permute-start(bf16[8,128]{1,0:T(8,128)(2,1)S(1)} %get-tuple-element.35), channel_id=1, source_target_pairs={{0,496},{8,504},{16,0},{24,8},{32,16},{40,24},{48,32},{56,40},{64,... | collective-permute-start | bytes 6152 | tf_op jit(solution)/shard_map/ppermute | solution.py:14
  18.6 35.9 %collective-permute-start.1 = (bf16[8,128]{1,0:T(8,128)(2,1)S(1)}, bf16[8,128]{1,0:T(8,128)(2,1)S(1)}, u32[]{:S(2)}, u32[]{:S(2)}) collective-permute-start(bf16[8,128]{1,0:T(8,128)(2,1)S(1)} %get-tuple-element.34), channel_id=1, source_target_pairs={{0,504},{8,0},{16,8},{24,16},{32,24},{40,32},{48,40},{56,48},{64,5... | collective-permute-start | bytes 6152 | tf_op jit(solution)/shard_map/ppermute | solution.py:14
  54.5 8.5 %collective-permute-start.2 = (bf16[8,128]{1,0:T(8,128)(2,1)S(1)}, bf16[8,128]{1,0:T(8,128)(2,1)S(1)}, u32[]{:S(2)}, u32[]{:S(2)}) collective-permute-start(bf16[8,128]{1,0:T(8,128)(2,1)S(1)} %get-tuple-element.32), channel_id=1, source_target_pairs={{0,8},{8,16},{16,24},{24,32},{32,40},{40,48},{48,56},{56,64},{64,7... | collective-permute-start | bytes 6152 | tf_op jit(solution)/shard_map/ppermute | solution.py:14
  56.6 9.1 %collective-permute-start.3 = (bf16[8,128]{1,0:T(8,128)(2,1)S(1)}, bf16[8,128]{1,0:T(8,128)(2,1)S(1)}, u32[]{:S(2)}, u32[]{:S(2)}) collective-permute-start(bf16[8,128]{1,0:T(8,128)(2,1)S(1)} %get-tuple-element.31), channel_id=1, source_target_pairs={{0,16},{8,24},{16,32},{24,40},{32,48},{40,56},{48,64},{56,72},{64,... | collective-permute-start | bytes 6152 | tf_op jit(solution)/shard_map/ppermute | solution.py:14
  94.5 11.0 %copy-start.5 = (s32[324]{0:T(512)S(1)}, s32[324]{0:T(512)}, u32[]{:S(2)}) copy-start(s32[324]{0:T(512)} %constant.224.clone) | copy-start | bytes 3892
  97.3 8.3 %collective-permute-start.4 = (bf16[64,2,60]{0,1,2:T(2,128)(2,1)S(1)}, bf16[64,2,60]{0,1,2:T(2,128)(2,1)S(1)}, u32[]{:S(2)}, u32[]{:S(2)}) collective-permute-start(bf16[64,2,60]{0,1,2:T(2,128)(2,1)S(1)} %get-tuple-element.29), channel_id=1, source_target_pairs={{0,1},{1,2},{2,3},{3,4},{4,5},{5,6},{6,7},{7,8},{8,9},{9,10},{10,1... | collective-permute-start | bytes 46088 | tf_op jit(solution)/shard_map/ppermute | solution.py:24
  100.6 6.3 %collective-permute-start.5 = (bf16[64,2,60]{0,1,2:T(2,128)(2,1)S(1)}, bf16[64,2,60]{0,1,2:T(2,128)(2,1)S(1)}, u32[]{:S(2)}, u32[]{:S(2)}) collective-permute-start(bf16[64,2,60]{0,1,2:T(2,128)(2,1)S(1)} %get-tuple-element.30), channel_id=1, source_target_pairs={{1,0},{2,1},{3,2},{4,3},{5,4},{6,5},{7,6},{8,7},{9,8},{10,9},{11,1... | collective-permute-start | bytes 46088 | tf_op jit(solution)/shard_map/ppermute | solution.py:25
  118.9 8.5 %collective-permute-start.6 = (bf16[128,2,60]{0,1,2:T(2,128)(2,1)S(1)}, bf16[128,2,60]{0,1,2:T(2,128)(2,1)S(1)}, u32[]{:S(2)}, u32[]{:S(2)}) collective-permute-start(bf16[128,2,60]{0,1,2:T(2,128)(2,1)S(1)} %get-tuple-element.27), channel_id=1, source_target_pairs={{0,1},{1,2},{2,3},{3,4},{4,5},{5,6},{6,7},{7,8},{8,9},{9,10},{10,1... | collective-permute-start | bytes 92168 | tf_op jit(solution)/shard_map/ppermute | solution.py:24
  121.5 7.3 %collective-permute-start.7 = (bf16[128,2,60]{0,1,2:T(2,128)(2,1)S(1)}, bf16[128,2,60]{0,1,2:T(2,128)(2,1)S(1)}, u32[]{:S(2)}, u32[]{:S(2)}) collective-permute-start(bf16[128,2,60]{0,1,2:T(2,128)(2,1)S(1)} %get-tuple-element.28), channel_id=1, source_target_pairs={{1,0},{2,1},{3,2},{4,3},{5,4},{6,5},{7,6},{8,7},{9,8},{10,9},{11,1... | collective-permute-start | bytes 92168 | tf_op jit(solution)/shard_map/ppermute | solution.py:25
  139.0 8.3 %collective-permute-start.8 = (bf16[128,2,60]{0,1,2:T(2,128)(2,1)S(1)}, bf16[128,2,60]{0,1,2:T(2,128)(2,1)S(1)}, u32[]{:S(2)}, u32[]{:S(2)}) collective-permute-start(bf16[128,2,60]{0,1,2:T(2,128)(2,1)S(1)} %get-tuple-element.25), channel_id=1, source_target_pairs={{0,1},{1,2},{2,3},{3,4},{4,5},{5,6},{6,7},{7,8},{8,9},{9,10},{10,1... | collective-permute-start | bytes 92168 | tf_op jit(solution)/shard_map/ppermute | solution.py:24
  141.5 7.4 %collective-permute-start.9 = (bf16[128,2,60]{0,1,2:T(2,128)(2,1)S(1)}, bf16[128,2,60]{0,1,2:T(2,128)(2,1)S(1)}, u32[]{:S(2)}, u32[]{:S(2)}) collective-permute-start(bf16[128,2,60]{0,1,2:T(2,128)(2,1)S(1)} %get-tuple-element.26), channel_id=1, source_target_pairs={{1,0},{2,1},{3,2},{4,3},{5,4},{6,5},{7,6},{8,7},{9,8},{10,9},{11,1... | collective-permute-start | bytes 92168 | tf_op jit(solution)/shard_map/ppermute | solution.py:25
where the time goes:
time: 178 us; the launch traced here: 177 us
  blocking collectives  76 us (43%)
  starting transfers between devices  45.7 us (26%)
  local copies, waits for them, and re-layouts  25.4 us (14%)
  matrix products  12.5 us (7%)
  waiting for transfers between devices  9.64 us (5%)
  other arithmetic  6.83 us (4%)
    all_gather x1, blocking collectives, on_device(): joined_kernels = lax.all_gather(joined_kernels, 'chan', axis=1, tiled=True)  29.9 us
    all_gather x1, blocking collectives, on_device(): arrived = lax.all_gather(arrived, 'chan', axis=0, tiled=True)  28.2 us
    ppermute x4, starting transfers between devices, from_behind(): return lax.ppermute(value, axis, pairs)  20.9 us
    all_to_all x1, blocking collectives, on_device(): lax.all_to_all(activity, 'chan', split_axis=0, concat_axis=1, tiled=True)  17.9 us
    ppermute x3, starting transfers between devices, extended_2(): after = lax.ppermute(initial, axis, down)  16.6 us
    dot_general x27, matrix products, conv_layer(): jnp.einsum('oc,ctq->otq', kernel[tap_index], window, preferred_element_ty...  10.1 us
    ppermute x3, starting transfers between devices, extended_2(): before = lax.ppermute(last, axis, up)  8.27 us
    gather x6, local copies, waits for them, and re-layouts, conv_layer(): padded = jnp.take(joined, layout_table(P_SIZE), axis=2)  6.41 us
  transfers between devices with their start and end apart: 10, of which 5 were waited for; matrix products, arithmetic and copies ran while one was open for 2% of the time, Pallas kernels for 0%

commit v1 on v0

--- a/solution.py
+++ b/solution.py
@@ -138,7 +138,13 @@
     per_group = tiles_here // groups
     widths = [kernel_one.shape[2], kernel_two.shape[2], kernel_three.shape[2]]
     joined_kernels = jnp.concatenate([kernel_one, kernel_two, kernel_three], axis=2)
-    joined_kernels = lax.all_gather(joined_kernels, "chan", axis=1, tiled=True)
+    lead_the_files = lambda packet: jnp.concatenate(
+        jax.lax.all_to_all(
+            jnp.stack([packet for _ in range(jax.lax.axis_size("chan"))]), "chan", 0, 0
+        ),
+        axis=1,
+    )
+    joined_kernels = lead_the_files(joined_kernels)
     kernels = []
     low = 0
     for width in widths:

time: 178 us -> 155 us (0.87)
  blocking collectives: 76 us -> 45.8 us
  starting transfers between devices: 45.7 us -> 52.2 us
    all_gather x1 -> x0, blocking collectives: 29.9 us -> none  [on_device(): joined_kernels = lax.all_gather(joined_kernels, 'chan', axis=1, tiled=True)]
    all_to_all x0 -> x1, starting transfers between devices: none -> 5.93 us  [on_device(): jax.lax.all_to_all(jnp.stack([packet for _ in range(jax.lax.axis_size('ch...]
  transfers between devices with their start and end apart: 10 -> 11, of which waited for: 5 -> 5; matrix products, arithmetic and copies ran while one was open for 2% -> 8% of each run, Pallas kernels for 0% -> 0%
where the time goes in v1:
time: 155 us; the launch traced here: 154 us
  starting transfers between devices  52.2 us (34%)
  blocking collectives  45.8 us (30%)
  local copies, waits for them, and re-layouts  26.5 us (17%)
  matrix products  12.5 us (8%)
  waiting for transfers between devices  9.13 us (6%)
  other arithmetic  6.81 us (4%)
    all_gather x1, blocking collectives, on_device(): arrived = lax.all_gather(arrived, 'chan', axis=0, tiled=True)  28.2 us
    ppermute x4, starting transfers between devices, from_behind(): return lax.ppermute(value, axis, pairs)  21.4 us
    ppermute x3, starting transfers between devices, extended_2(): after = lax.ppermute(initial, axis, down)  18.1 us
    all_to_all x1, blocking collectives, on_device(): lax.all_to_all(activity, 'chan', split_axis=0, concat_axis=1, tiled=True)  17.6 us
    dot_general x27, matrix products, conv_layer(): jnp.einsum('oc,ctq->otq', kernel[tap_index], window, preferred_element_ty...  10.1 us
    ppermute x3, starting transfers between devices, extended_2(): before = lax.ppermute(last, axis, up)  6.77 us
    gather x6, local copies, waits for them, and re-layouts, conv_layer(): padded = jnp.take(joined, layout_table(P_SIZE), axis=2)  6.41 us
    all_to_all x1, starting transfers between devices, on_device(): jax.lax.all_to_all(jnp.stack([packet for _ in range(jax.lax.axis_size('ch...  5.93 us
  transfers between devices with their start and end apart: 11, of which 5 were waited for; matrix products, arithmetic and copies ran while one was open for 8% of the time, Pallas kernels for 0%

profile of v1, /device:TPU:2, one launch (start us, length us, event | category | flops | bytes accessed | tf_op | source)
XLA Modules:
  0.0 154.0 jit_solution(834901621001761742)
XLA Ops:
  0.8 0.8 iota_compare_fusion.24
  1.5 1.9 %copy.221 = bf16[8,8192]{0,1:T(8,128)(2,1)S(1)} copy(bf16[8,8192]{1,0:T(8,128)(2,1)} %param.30) | data formatting | bytes 262144 | tf_op args[0]
  3.5 2.0 %gather_fusion = bf16[640,8]{1,0:T(8,128)(2,1)S(1)} fusion(bf16[8,8192]{0,1:T(8,128)(2,1)S(1)} %copy.221, s32[1024]{0:T(1024)S(1)} %pad_clamp_fusion.5), kind=kCustom, calls=%fused_computation.8 | custom fusion | bytes 23040 | tf_op jit(solution)/shard_map/jit(_take)/gather | solution.py:155
  5.6 13.0 %collective-permute-start = (bf16[8,128]{1,0:T(8,128)(2,1)S(1)}, bf16[8,128]{1,0:T(8,128)(2,1)S(1)}, u32[]{:S(2)}, u32[]{:S(2)}) collective-permute-start(bf16[8,128]{1,0:T(8,128)(2,1)S(1)} %get-tuple-element.35), channel_id=1, source_target_pairs={{0,496},{8,504},{16,0},{24,8},{32,16},{40,24},{48,32},{56,40},{64,... | collective-permute-start | bytes 6152 | tf_op jit(solution)/shard_map/ppermute | solution.py:14
  18.6 2.5 %collective-permute-start.1 = (bf16[8,128]{1,0:T(8,128)(2,1)S(1)}, bf16[8,128]{1,0:T(8,128)(2,1)S(1)}, u32[]{:S(2)}, u32[]{:S(2)}) collective-permute-start(bf16[8,128]{1,0:T(8,128)(2,1)S(1)} %get-tuple-element.34), channel_id=1, source_target_pairs={{0,504},{8,0},{16,8},{24,16},{32,24},{40,32},{48,40},{56,48},{64,5... | collective-permute-start | bytes 6152 | tf_op jit(solution)/shard_map/ppermute | solution.py:14
  21.2 1.0 stack.12
  22.2 5.9 %all-to-all-start = ((bf16[8,9,16,320]{3,2,1,0:T(8,128)(2,1)}), bf16[8,9,16,320]{3,2,1,0:T(8,128)(2,1)S(1)}, u32[]{:S(2)}, u32[]{:S(2)}) async-start(bf16[8,9,16,320]{3,2,1,0:T(8,128)(2,1)} %stack.12), calls=%async_computation | async-start | bytes 1769472 | tf_op jit(solution)/shard_map/all_to_all | solution.py:142
  31.5 1.9 %collective-permute-start.2 = (bf16[8,128]{1,0:T(8,128)(2,1)S(1)}, bf16[8,128]{1,0:T(8,128)(2,1)S(1)}, u32[]{:S(2)}, u32[]{:S(2)}) collective-permute-start(bf16[8,128]{1,0:T(8,128)(2,1)S(1)} %get-tuple-element.32), channel_id=1, source_target_pairs={{0,8},{8,16},{16,24},{24,32},{32,40},{40,48},{48,56},{56,64},{64,7... | collective-permute-start | bytes 6152 | tf_op jit(solution)/shard_map/ppermute | solution.py:14
  33.5 4.0 %collective-permute-start.3 = (bf16[8,128]{1,0:T(8,128)(2,1)S(1)}, bf16[8,128]{1,0:T(8,128)(2,1)S(1)}, u32[]{:S(2)}, u32[]{:S(2)}) collective-permute-start(bf16[8,128]{1,0:T(8,128)(2,1)S(1)} %get-tuple-element.31), channel_id=1, source_target_pairs={{0,16},{8,24},{16,32},{24,40},{32,48},{40,56},{48,64},{56,72},{64,... | collective-permute-start | bytes 6152 | tf_op jit(solution)/shard_map/ppermute | solution.py:14
  37.6 2.4 %collective-permute-done.2 = bf16[8,128]{1,0:T(8,128)(2,1)S(1)} collective-permute-done((bf16[8,128]{1,0:T(8,128)(2,1)S(1)}, bf16[8,128]{1,0:T(8,128)(2,1)S(1)}, u32[]{:S(2)}, u32[]{:S(2)}) %collective-permute-start.2) | collective-permute-done | bytes 2080 | tf_op jit(solution)/shard_map/ppermute | solution.py:14
  40.0 2.6 %collective-permute-done.3 = bf16[8,128]{1,0:T(8,128)(2,1)S(1)} collective-permute-done((bf16[8,128]{1,0:T(8,128)(2,1)S(1)}, bf16[8,128]{1,0:T(8,128)(2,1)S(1)}, u32[]{:S(2)}, u32[]{:S(2)}) %collective-permute-start.3) | collective-permute-done | bytes 2080 | tf_op jit(solution)/shard_map/ppermute | solution.py:14
  42.6 28.2 %all_gather.3 = bf16[64,640]{1,0:T(8,128)(2,1)S(1)} all-gather(bf16[8,640]{1,0:T(8,128)(2,1)S(1)} %bitcast.302), channel_id=1, replica_groups=mesh['tile'=64,'chan'=8] {'chan'}, dimensions={0}, use_global_device_ids=true | all-gather | bytes 92160 | tf_op jit(solution)/shard_map/all_gather | solution.py:165
  74.3 2.5 %collective-permute-start.4 = (bf16[64,2,60]{0,1,2:T(2,128)(2,1)S(1)}, bf16[64,2,60]{0,1,2:T(2,128)(2,1)S(1)}, u32[]{:S(2)}, u32[]{:S(2)}) collective-permute-start(bf16[64,2,60]{0,1,2:T(2,128)(2,1)S(1)} %get-tuple-element.29), channel_id=1, source_target_pairs={{0,1},{1,2},{2,3},{3,4},{4,5},{5,6},{6,7},{7,8},{8,9},{9,10},{10,1... | collective-permute-start | bytes 46088 | tf_op jit(solution)/shard_map/ppermute | solution.py:24
  76.8 5.6 %collective-permute-start.5 = (bf16[64,2,60]{0,1,2:T(2,128)(2,1)S(1)}, bf16[64,2,60]{0,1,2:T(2,128)(2,1)S(1)}, u32[]{:S(2)}, u32[]{:S(2)}) collective-permute-start(bf16[64,2,60]{0,1,2:T(2,128)(2,1)S(1)} %get-tuple-element.30), channel_id=1, source_target_pairs={{1,0},{2,1},{3,2},{4,3},{5,4},{6,5},{7,6},{8,7},{9,8},{10,9},{11,1... | collective-permute-start | bytes 46088 | tf_op jit(solution)/shard_map/ppermute | solution.py:25
  82.6 1.2 collective-permute-done.5
  84.0 1.4 gather_fusion.2
  85.9 2.0 %gather_fusion.3 = bf16[324,64,4]{1,2,0:T(4,128)(2,1)S(1)} fusion(bf16[64,4,324]{0,1,2:T(4,128)(2,1)S(1)} %pad_maximum_fusion.2, s32[1024]{0:T(1024)S(1)} %get-tuple-element.37), kind=kCustom, calls=%fused_computation.11 | custom fusion | bytes 333072 | tf_op jit(solution)/shard_map/jit(_take)/gather | solution.py:101
  94.0 1.1 fusion.18
  96.0 2.2 %collective-permute-start.6 = (bf16[128,2,60]{0,1,2:T(2,128)(2,1)S(1)}, bf16[128,2,60]{0,1,2:T(2,128)(2,1)S(1)}, u32[]{:S(2)}, u32[]{:S(2)}) collective-permute-start(bf16[128,2,60]{0,1,2:T(2,128)(2,1)S(1)} %get-tuple-element.27), channel_id=1, source_target_pairs={{0,1},{1,2},{2,3},{3,4},{4,5},{5,6},{6,7},{7,8},{8,9},{9,10},{10,1... | collective-permute-start | bytes 92168 | tf_op jit(solution)/shard_map/ppermute | solution.py:24
  98.1 6.3 %collective-permute-start.7 = (bf16[128,2,60]{0,1,2:T(2,128)(2,1)S(1)}, bf16[128,2,60]{0,1,2:T(2,128)(2,1)S(1)}, u32[]{:S(2)}, u32[]{:S(2)}) collective-permute-start(bf16[128,2,60]{0,1,2:T(2,128)(2,1)S(1)} %get-tuple-element.28), channel_id=1, source_target_pairs={{1,0},{2,1},{3,2},{4,3},{5,4},{6,5},{7,6},{8,7},{9,8},{10,9},{11,1... | collective-permute-start | bytes 92168 | tf_op jit(solution)/shard_map/ppermute | solution.py:25
  104.5 1.3 collective-permute-done.7
  106.0 1.4 gather_fusion.7
  107.9 2.0 %gather_fusion.8 = bf16[324,128,4]{1,2,0:T(4,128)(2,1)S(1)} fusion(bf16[128,4,324]{0,1,2:T(4,128)(2,1)S(1)} %copy.253, s32[1024]{0:T(1024)S(1)} %get-tuple-element.37), kind=kCustom, calls=%fused_computation.3.clone | custom fusion | bytes 664848 | tf_op jit(solution)/shard_map/jit(_take)/gather | solution.py:101
  114.1 1.1 fusion.21
  116.1 2.1 %collective-permute-start.8 = (bf16[128,2,60]{0,1,2:T(2,128)(2,1)S(1)}, bf16[128,2,60]{0,1,2:T(2,128)(2,1)S(1)}, u32[]{:S(2)}, u32[]{:S(2)}) collective-permute-start(bf16[128,2,60]{0,1,2:T(2,128)(2,1)S(1)} %get-tuple-element.25), channel_id=1, source_target_pairs={{0,1},{1,2},{2,3},{3,4},{4,5},{5,6},{6,7},{7,8},{8,9},{9,10},{10,1... | collective-permute-start | bytes 92168 | tf_op jit(solution)/shard_map/ppermute | solution.py:24
  118.2 6.2 %collective-permute-start.9 = (bf16[128,2,60]{0,1,2:T(2,128)(2,1)S(1)}, bf16[128,2,60]{0,1,2:T(2,128)(2,1)S(1)}, u32[]{:S(2)}, u32[]{:S(2)}) collective-permute-start(bf16[128,2,60]{0,1,2:T(2,128)(2,1)S(1)} %get-tuple-element.26), channel_id=1, source_target_pairs={{1,0},{2,1},{3,2},{4,3},{5,4},{6,5},{7,6},{8,7},{9,8},{10,9},{11,1... | collective-permute-start | bytes 92168 | tf_op jit(solution)/shard_map/ppermute | solution.py:25
  124.4 1.5 %collective-permute-done.9 = bf16[128,2,60]{0,1,2:T(2,128)(2,1)S(1)} collective-permute-done((bf16[128,2,60]{0,1,2:T(2,128)(2,1)S(1)}, bf16[128,2,60]{0,1,2:T(2,128)(2,1)S(1)}, u32[]{:S(2)}, u32[]{:S(2)}) %collective-permute-start.9) | collective-permute-done | bytes 30752 | tf_op jit(solution)/shard_map/ppermute | solution.py:25
  126.1 1.4 gather_fusion.10
  128.1 2.0 %gather_fusion.11 = bf16[324,128,4]{1,2,0:T(4,128)(2,1)S(1)} fusion(bf16[128,4,324]{0,1,2:T(4,128)(2,1)S(1)} %copy.267, s32[1024]{0:T(1024)S(1)} %get-tuple-element.37), kind=kCustom, calls=%fused_computation.7.clone | custom fusion | bytes 664848 | tf_op jit(solution)/shard_map/jit(_take)/gather | solution.py:101
  134.2 1.1 fusion.24
  135.5 17.6 %all_to_all.23 = bf16[128,4,256]{2,1,0:T(4,128)(2,1)S(1)} all-to-all(bf16[128,4,256]{2,1,0:T(4,128)(2,1)S(1)} %copy.278), channel_id=1, replica_groups=mesh['tile'=64,'chan'=8] {'chan'}, dimensions={0} | all-to-all | bytes 524288 | tf_op jit(solution)/shard_map/all_to_all | solution.py:189
  153.2 0.8 copy.281
  (149 shorter events, 26.0 us)
Async XLA Ops:
  0.0 28.9 %copy-start = (s32[32,8]{0,1:T(8,128)S(1)}, s32[32,8]{0,1:T(8,128)}, u32[]{:S(2)}) copy-start(s32[32,8]{0,1:T(8,128)} %param.36) | copy-start | bytes 3076
  0.0 21.1 %copy-start.3 = (bf16[9,16,64]{2,1,0:T(8,128)(2,1)S(1)}, bf16[9,16,64]{2,1,0:T(8,128)(2,1)}, u32[]{:S(2)}) copy-start(bf16[9,16,64]{2,1,0:T(8,128)(2,1)} %param.37) | copy-start | bytes 55300
  0.0 21.1 %copy-start.2 = (bf16[9,16,128]{2,1,0:T(8,128)(2,1)S(1)}, bf16[9,16,128]{2,1,0:T(8,128)(2,1)}, u32[]{:S(2)}) copy-start(bf16[9,16,128]{2,1,0:T(8,128)(2,1)} %param.38) | copy-start | bytes 110596
  0.0 21.1 %copy-start.1 = (bf16[9,16,128]{2,1,0:T(8,128)(2,1)S(1)}, bf16[9,16,128]{2,1,0:T(8,128)(2,1)}, u32[]{:S(2)}) copy-start(bf16[9,16,128]{2,1,0:T(8,128)(2,1)} %param.39) | copy-start | bytes 110596
  3.4 24.7 %copy-start.7 = (s32[68]{0:T(128)S(1)}, s32[68]{0:T(128)}, u32[]{:S(2)}) copy-start(s32[68]{0:T(128)} %constant.310) | copy-start | bytes 820
  3.4 24.7 %copy-start.4 = (s32[32,8]{0,1:T(8,128)S(1)}, s32[32,8]{0,1:T(8,128)}, u32[]{:S(2)}) copy-start(s32[32,8]{0,1:T(8,128)} %param.35) | copy-start | bytes 3076
  3.4 26.3 %copy-start.6 = (s32[68]{0:T(128)S(1)}, s32[68]{0:T(128)}, u32[]{:S(2)}) copy-start(s32[68]{0:T(128)} %constant.243) | copy-start | bytes 820
  3.5 30.0 %copy-start.8 = (s32[60]{0:T(128)S(1)}, s32[60]{0:T(128)}, u32[]{:S(2)}) copy-start(s32[60]{0:T(128)} %constant.221.clone) | copy-start | bytes 724
  5.6 25.8 %collective-permute-start = (bf16[8,128]{1,0:T(8,128)(2,1)S(1)}, bf16[8,128]{1,0:T(8,128)(2,1)S(1)}, u32[]{:S(2)}, u32[]{:S(2)}) collective-permute-start(bf16[8,128]{1,0:T(8,128)(2,1)S(1)} %get-tuple-element.35), channel_id=1, source_target_pairs={{0,496},{8,504},{16,0},{24,8},{32,16},{40,24},{48,32},{56,40},{64,... | collective-permute-start | bytes 6152 | tf_op jit(solution)/shard_map/ppermute | solution.py:14
  18.6 12.9 %collective-permute-start.1 = (bf16[8,128]{1,0:T(8,128)(2,1)S(1)}, bf16[8,128]{1,0:T(8,128)(2,1)S(1)}, u32[]{:S(2)}, u32[]{:S(2)}) collective-permute-start(bf16[8,128]{1,0:T(8,128)(2,1)S(1)} %get-tuple-element.34), channel_id=1, source_target_pairs={{0,504},{8,0},{16,8},{24,16},{32,24},{40,32},{48,40},{56,48},{64,5... | collective-permute-start | bytes 6152 | tf_op jit(solution)/shard_map/ppermute | solution.py:14
  22.2 65.9 %all-to-all-start = ((bf16[8,9,16,320]{3,2,1,0:T(8,128)(2,1)}), bf16[8,9,16,320]{3,2,1,0:T(8,128)(2,1)S(1)}, u32[]{:S(2)}, u32[]{:S(2)}) async-start(bf16[8,9,16,320]{3,2,1,0:T(8,128)(2,1)} %stack.12), calls=%async_computation | async-start | bytes 1769472 | tf_op jit(solution)/shard_map/all_to_all | solution.py:142
  31.5 8.5 %collective-permute-start.2 = (bf16[8,128]{1,0:T(8,128)(2,1)S(1)}, bf16[8,128]{1,0:T(8,128)(2,1)S(1)}, u32[]{:S(2)}, u32[]{:S(2)}) collective-permute-start(bf16[8,128]{1,0:T(8,128)(2,1)S(1)} %get-tuple-element.32), channel_id=1, source_target_pairs={{0,8},{8,16},{16,24},{24,32},{32,40},{40,48},{48,56},{56,64},{64,7... | collective-permute-start | bytes 6152 | tf_op jit(solution)/shard_map/ppermute | solution.py:14
  33.5 9.1 %collective-permute-start.3 = (bf16[8,128]{1,0:T(8,128)(2,1)S(1)}, bf16[8,128]{1,0:T(8,128)(2,1)S(1)}, u32[]{:S(2)}, u32[]{:S(2)}) collective-permute-start(bf16[8,128]{1,0:T(8,128)(2,1)S(1)} %get-tuple-element.31), channel_id=1, source_target_pairs={{0,16},{8,24},{16,32},{24,40},{32,48},{40,56},{48,64},{56,72},{64,... | collective-permute-start | bytes 6152 | tf_op jit(solution)/shard_map/ppermute | solution.py:14
  71.4 11.0 %copy-start.5 = (s32[324]{0:T(512)S(1)}, s32[324]{0:T(512)}, u32[]{:S(2)}) copy-start(s32[324]{0:T(512)} %constant.224.clone) | copy-start | bytes 3892
  74.3 8.3 %collective-permute-start.4 = (bf16[64,2,60]{0,1,2:T(2,128)(2,1)S(1)}, bf16[64,2,60]{0,1,2:T(2,128)(2,1)S(1)}, u32[]{:S(2)}, u32[]{:S(2)}) collective-permute-start(bf16[64,2,60]{0,1,2:T(2,128)(2,1)S(1)} %get-tuple-element.29), channel_id=1, source_target_pairs={{0,1},{1,2},{2,3},{3,4},{4,5},{5,6},{6,7},{7,8},{8,9},{9,10},{10,1... | collective-permute-start | bytes 46088 | tf_op jit(solution)/shard_map/ppermute | solution.py:24
  76.8 7.0 %collective-permute-start.5 = (bf16[64,2,60]{0,1,2:T(2,128)(2,1)S(1)}, bf16[64,2,60]{0,1,2:T(2,128)(2,1)S(1)}, u32[]{:S(2)}, u32[]{:S(2)}) collective-permute-start(bf16[64,2,60]{0,1,2:T(2,128)(2,1)S(1)} %get-tuple-element.30), channel_id=1, source_target_pairs={{1,0},{2,1},{3,2},{4,3},{5,4},{6,5},{7,6},{8,7},{9,8},{10,9},{11,1... | collective-permute-start | bytes 46088 | tf_op jit(solution)/shard_map/ppermute | solution.py:25
  96.0 8.5 %collective-permute-start.6 = (bf16[128,2,60]{0,1,2:T(2,128)(2,1)S(1)}, bf16[128,2,60]{0,1,2:T(2,128)(2,1)S(1)}, u32[]{:S(2)}, u32[]{:S(2)}) collective-permute-start(bf16[128,2,60]{0,1,2:T(2,128)(2,1)S(1)} %get-tuple-element.27), channel_id=1, source_target_pairs={{0,1},{1,2},{2,3},{3,4},{4,5},{5,6},{6,7},{7,8},{8,9},{9,10},{10,1... | collective-permute-start | bytes 92168 | tf_op jit(solution)/shard_map/ppermute | solution.py:24
  98.1 7.6 %collective-permute-start.7 = (bf16[128,2,60]{0,1,2:T(2,128)(2,1)S(1)}, bf16[128,2,60]{0,1,2:T(2,128)(2,1)S(1)}, u32[]{:S(2)}, u32[]{:S(2)}) collective-permute-start(bf16[128,2,60]{0,1,2:T(2,128)(2,1)S(1)} %get-tuple-element.28), channel_id=1, source_target_pairs={{1,0},{2,1},{3,2},{4,3},{5,4},{6,5},{7,6},{8,7},{9,8},{10,9},{11,1... | collective-permute-start | bytes 92168 | tf_op jit(solution)/shard_map/ppermute | solution.py:25
  116.1 8.3 %collective-permute-start.8 = (bf16[128,2,60]{0,1,2:T(2,128)(2,1)S(1)}, bf16[128,2,60]{0,1,2:T(2,128)(2,1)S(1)}, u32[]{:S(2)}, u32[]{:S(2)}) collective-permute-start(bf16[128,2,60]{0,1,2:T(2,128)(2,1)S(1)} %get-tuple-element.25), channel_id=1, source_target_pairs={{0,1},{1,2},{2,3},{3,4},{4,5},{5,6},{6,7},{7,8},{8,9},{9,10},{10,1... | collective-permute-start | bytes 92168 | tf_op jit(solution)/shard_map/ppermute | solution.py:24
  118.2 7.8 %collective-permute-start.9 = (bf16[128,2,60]{0,1,2:T(2,128)(2,1)S(1)}, bf16[128,2,60]{0,1,2:T(2,128)(2,1)S(1)}, u32[]{:S(2)}, u32[]{:S(2)}) collective-permute-start(bf16[128,2,60]{0,1,2:T(2,128)(2,1)S(1)} %get-tuple-element.26), channel_id=1, source_target_pairs={{1,0},{2,1},{3,2},{4,3},{5,4},{6,5},{7,6},{8,7},{9,8},{10,9},{11,1... | collective-permute-start | bytes 92168 | tf_op jit(solution)/shard_map/ppermute | solution.py:25
